TPU v7x, 512 devices: a whole 4x4x16 slice. The times are simulated.
512 devices in a mesh: cand: 8 (over y, core), doc: 64 (over z, x).
Axes of the slice: x: 4, y: 4, z: 16, core: 2. Of those that a mesh axis runs over, the one named last changes fastest.
Arguments:
- queries: bfloat16 [8192, 8192], P('doc'), may hold values from -6 to 50
- keys_values: bfloat16 [2, 8192, 1024], P(None, 'doc', 'cand'), may hold values from -6 to 50
- factors: float32 [8, 64], P('cand'), may hold values from 1 to 16
- lengths: int32 [16], replicated, may hold values from 1 to 1024, 8192 in all
Outputs:
- attended: bfloat16 [8, 8192, 8192], P('cand', 'doc')
All inputs are finite; a program needn't handle non-finite values.
Results may differ from a plain program's by a relative error of at most 0.0053.
Values may be sent and summed in bfloat16 or wider, within the bound.
No kernel may reach another device: no remote copies, remote signals or barrier semaphores. Data moves between devices by JAX's collectives and lax.ppermute only.
A program may use at most 64 MiB of HBM per device.

v0:
```python
import math
import jax
import jax.numpy as jnp
from jax import lax
from jax.sharding import PartitionSpec as P

H = 64
KVH = 8
HD = 128
SPAN = 8
ROPE_BASE = 500000.0


def passed_along(value, axis, steps):
    count = lax.axis_size(axis)
    first, last = (max(0, -steps), min(count, count - steps))
    return lax.ppermute(value, axis, [(source, source + steps) for source in range(first, last)])


def locate(index_rows, lengths):
    ends = jnp.cumsum(lengths)
    starts = ends - lengths
    docid = jnp.sum((index_rows[:, None] >= ends[None, :]).astype(jnp.int32), axis=1)
    onehot = docid[:, None] == jnp.arange(lengths.shape[0], dtype=jnp.int32)[None, :]
    first_row = jnp.sum(jnp.where(onehot, starts[None, :], 0), axis=1)
    valid = index_rows >= 0
    return (jnp.where(valid, docid, -1), jnp.where(valid, index_rows - first_row, 0))


def rotate(values, offsets, factor):
    row_count = values.shape[0]
    heads_here = values.shape[1] // HD
    half_dim = HD // 2
    shaped = values.reshape(row_count, heads_here, HD).astype(jnp.float32)
    inverse = jnp.power(ROPE_BASE, -2.0 * jnp.arange(half_dim, dtype=jnp.float32) / HD) / factor
    angles = offsets.astype(jnp.float32)[:, None] * inverse[None, :]
    cosine = jnp.cos(angles)[:, None, :]
    sine = jnp.sin(angles)[:, None, :]
    first_half = shaped[..., :half_dim]
    second_half = shaped[..., half_dim:]
    turned = jnp.concatenate(
        [first_half * cosine - second_half * sine, second_half * cosine + first_half * sine],
        axis=-1,
    )
    return turned.reshape(row_count, heads_here * HD).astype(jnp.bfloat16)


def attend(query_rot, key_rot, value_rows, query_doc, query_index, key_doc, key_index):
    row_count = query_rot.shape[0]
    key_count = key_rot.shape[0]
    group_size = H // KVH
    q_grouped = query_rot.reshape(row_count, KVH, group_size, HD).transpose(1, 0, 2, 3)
    k_grouped = key_rot.reshape(key_count, KVH, HD).transpose(1, 0, 2)
    v_grouped = value_rows.reshape(key_count, KVH, HD).transpose(1, 0, 2)
    allowed = (
        (key_doc[None, :] == query_doc[:, None])
        & (key_index[None, :] <= query_index[:, None])
        & (key_doc[None, :] >= 0)
    )
    scale = 1.0 / math.sqrt(HD)

    def per_group(operands):
        q_part, k_part, v_part = operands
        scores = (
            jnp.einsum("rgd,wd->rgw", q_part, k_part, preferred_element_type=jnp.float32) * scale
        )
        scores = jnp.where(allowed[:, None, :], scores, -1e30)
        largest = jnp.max(scores, axis=-1, keepdims=True)
        expw = jnp.exp(scores - largest)
        total = jnp.sum(expw, axis=-1, keepdims=True)
        weights = expw.astype(jnp.bfloat16)
        numer = jnp.einsum("rgw,wd->rgd", weights, v_part, preferred_element_type=jnp.float32)
        return (numer / total).astype(jnp.bfloat16)

    mixed = lax.map(per_group, (q_grouped, k_grouped, v_grouped))
    return mixed.transpose(1, 0, 2, 3).reshape(row_count, H * HD)


def on_device(queries, keys_values, factors, lengths):
    row_count = queries.shape[0]
    device = lax.axis_index("doc")
    query_index = device * row_count + jnp.arange(row_count, dtype=jnp.int32)
    key_index = (device - SPAN) * row_count + jnp.arange((SPAN + 1) * row_count, dtype=jnp.int32)
    whole = lax.all_gather(keys_values, "cand", axis=2, tiled=True)
    pieces = []
    for distance in range(SPAN, 0, -1):
        pieces.append(passed_along(whole, "doc", distance))
    pieces.append(whole)
    window = jnp.concatenate(pieces, axis=1)
    query_doc, query_offset = locate(query_index, lengths)
    key_doc, key_offset = locate(key_index, lengths)
    factor = factors[0]
    query_rot = rotate(queries, query_offset, factor)
    key_rot = rotate(window[0], key_offset, factor)
    mixed = attend(query_rot, key_rot, window[1], query_doc, query_index, key_doc, key_index)
    return mixed[None]


def solution(mesh):
    placed = (P("doc", None), P(None, "doc", "cand"), P("cand", None), P())
    return jax.shard_map(
        on_device, mesh=mesh, in_specs=placed, out_specs=P("cand", "doc", None), check_vma=False
    )
```

profile of v0, /device:TPU:448, one launch (start us, length us, event | category | flops | bytes accessed | tf_op | source)
XLA Modules:
  0.0 222.4 jit_solution(7817300378528015322)
XLA Ops:
  0.0 0.9 copy.19
  1.0 13.6 %all_gather.3 = bf16[2,128,1024]{1,2,0:T(8,128)(2,1)S(1)} all-gather(bf16[2,128,128]{1,2,0:T(8,128)(2,1)S(1)} %copy.19), channel_id=1, replica_groups=mesh['cand'=8,'doc'=64] {'cand'}, dimensions={2}, use_global_device_ids=true | all-gather | bytes 589824 | tf_op jit(solution)/shard_map/all_gather | solution.py:84
  14.6 1.3 collective-permute-start
  15.9 5.1 %collective-permute-start.1 = (bf16[2,128,1024]{1,2,0:T(8,128)(2,1)S(1)}, bf16[2,128,1024]{1,2,0:T(8,128)(2,1)S(1)}, u32[]{:S(2)}, u32[]{:S(2)}) collective-permute-start(bf16[2,128,1024]{1,2,0:T(8,128)(2,1)S(1)} %all_gather.3), channel_id=1, source_target_pairs={{0,7},{1,8},{2,9},{3,10},{4,11},{5,12},{6,13},{7,14},{8,15},{9,16}... | collective-permute-start | bytes 1572872 | tf_op jit(solution)/shard_map/ppermute | solution.py:17
  21.0 1.9 collective-permute-start.2
  22.9 1.9 collective-permute-start.3
  24.9 1.9 collective-permute-start.4
  26.8 2.0 convert_bitcast_fusion
  28.8 0.7 copy.27
  29.6 4.6 %fusion.35 = (f32[128,64,64]{2,1,0:T(8,128)}, f32[128,64,64]{2,1,0:T(8,128)}) fusion(f32[128,64,128]{2,1,0:T(8,128)S(1)} %bitcast.48), kind=kLoop, calls=%fused_computation.60 | loop fusion | bytes 8388608 | tf_op jit(solution)/shard_map/slice | solution.py:39
  34.8 0.3 multiply_cosine_fusion.1
  35.1 8.3 %subtract_convert_fusion = (bf16[128,64,64]{2,0,1:T(8,128)(2,1)S(1)}, bf16[128,64,64]{2,0,1:T(8,128)(2,1)S(1)}) fusion(f32[128,64,64]{2,1,0:T(8,128)} %get-tuple-element.116, f32[128,64,64]{2,1,0:T(8,128)} %get-tuple-element.115, f32[128,64]{1,0:T(8,128)S(1)} %get-tuple-element.120, f32[128,64]{1,0:T(8,128)S(1)} %get-tuple-element.119), kind=kLoop, calls=%fused_computation.23 | loop fusion | flops 4194304 | bytes 6356992 | tf_op jit(solution)/shard_map/convert.4
  43.5 1.1 multiply_cosine_fusion
  44.6 2.5 %pad_maximum_fusion = bf16[128,64,128]{2,0,1:T(8,128)(2,1)} fusion(bf16[128,64,64]{2,0,1:T(8,128)(2,1)S(1)} %get-tuple-element.110, bf16[128,64,64]{2,0,1:T(8,128)(2,1)S(1)} %get-tuple-element.109), kind=kLoop, calls=%fused_computation.27 | loop fusion | flops 4194304 | bytes 4194304 | tf_op jit(solution)/shard_map/concatenate | solution.py:41
  47.1 2.1 collective-permute-start.5
  49.2 1.1 constant_dynamic-update-slice_fusion.8
  50.3 16.4 %collective-permute-done.1 = bf16[2,128,1024]{1,2,0:T(8,128)(2,1)S(1)} collective-permute-done((bf16[2,128,1024]{1,2,0:T(8,128)(2,1)S(1)}, bf16[2,128,1024]{1,2,0:T(8,128)(2,1)S(1)}, u32[]{:S(2)}, u32[]{:S(2)}) %collective-permute-start.1) | collective-permute-done | bytes 524320 | tf_op jit(solution)/shard_map/ppermute | solution.py:17
  66.7 1.9 collective-permute-start.6
  68.7 0.1 constant_dynamic-update-slice_fusion.7
  68.8 22.0 %collective-permute-done.2 = bf16[2,128,1024]{1,2,0:T(8,128)(2,1)S(1)} collective-permute-done((bf16[2,128,1024]{1,2,0:T(8,128)(2,1)S(1)}, bf16[2,128,1024]{1,2,0:T(8,128)(2,1)S(1)}, u32[]{:S(2)}, u32[]{:S(2)}) %collective-permute-start.2) | collective-permute-done | bytes 524320 | tf_op jit(solution)/shard_map/ppermute | solution.py:17
  90.8 1.9 collective-permute-start.7
  92.9 20.1 %collective-permute-done.3 = bf16[2,128,1024]{1,2,0:T(8,128)(2,1)S(1)} collective-permute-done((bf16[2,128,1024]{1,2,0:T(8,128)(2,1)S(1)}, bf16[2,128,1024]{1,2,0:T(8,128)(2,1)S(1)}, u32[]{:S(2)}, u32[]{:S(2)}) %collective-permute-start.3) | collective-permute-done | bytes 524320 | tf_op jit(solution)/shard_map/ppermute | solution.py:17
  113.2 6.8 %collective-permute-done.5 = bf16[2,128,1024]{1,2,0:T(8,128)(2,1)S(1)} collective-permute-done((bf16[2,128,1024]{1,2,0:T(8,128)(2,1)S(1)}, bf16[2,128,1024]{1,2,0:T(8,128)(2,1)S(1)}, u32[]{:S(2)}, u32[]{:S(2)}) %collective-permute-start.5) | collective-permute-done | bytes 524320 | tf_op jit(solution)/shard_map/ppermute | solution.py:17
  120.1 14.6 %collective-permute-done.6 = bf16[2,128,1024]{1,2,0:T(8,128)(2,1)S(1)} collective-permute-done((bf16[2,128,1024]{1,2,0:T(8,128)(2,1)S(1)}, bf16[2,128,1024]{1,2,0:T(8,128)(2,1)S(1)}, u32[]{:S(2)}, u32[]{:S(2)}) %collective-permute-start.6) | collective-permute-done | bytes 524320 | tf_op jit(solution)/shard_map/ppermute | solution.py:17
  134.9 31.8 %collective-permute-done.7 = bf16[2,128,1024]{1,2,0:T(8,128)(2,1)S(1)} collective-permute-done((bf16[2,128,1024]{1,2,0:T(8,128)(2,1)S(1)}, bf16[2,128,1024]{1,2,0:T(8,128)(2,1)S(1)}, u32[]{:S(2)}, u32[]{:S(2)}) %collective-permute-start.7) | collective-permute-done | bytes 524320 | tf_op jit(solution)/shard_map/ppermute | solution.py:17
  166.9 1.8 fusion.34
  168.7 0.3 convert.18
  169.0 0.6 subtract_convert_fusion.1
  169.7 0.2 maximum_bitcast_fusion
  169.9 47.3 %while.11 = (s32[]{:T(128)}, bf16[8,128,8,128]{3,1,2,0:T(8,128)(2,1)}, bf16[8,128,8,128]{3,1,2,0:T(8,128)(2,1)}, bf16[8,1152,128]{1,2,0:T(8,128)(2,1)S(1)}, bf16...) while((s32[]{:T(128)}, ...), condition=%wide.region_8.9_spmd.clone, body=%wide.region_5.8_spmd.clone.sunk | while | flops 613087232 | bytes 15598837 | solution.py:75
  169.9 0.2 and_and_fusion.2
  170.1 2.1 fusion.43
  172.2 1.0 fusion.44
  173.2 2.6 %fusion.45 = bf16[8,128,8,128]{3,1,2,0:T(8,128)(2,1)} fusion(bf16[8,128,8,128]{3,1,2,0:T(8,128)(2,1)} %get-tuple-element.200, s32[]{:T(128)S(6)} %copy.43, f32[128,8,1152]{2,0,1:T(8,128)S(1)} %get-tuple-element.186, f32[128,8]{0,1:T(8,128)S(1)} %get-tuple-element.187, bf16[8,1152,128]{1,2,0:T(8,128)(2,1)} %get-tuple-element.214, ...), kind=kOutput, calls=%fused_computation.11.clone.1 | convolution fusion | flops 304611328 | bytes 5284864 | tf_op jit(solution)/shard_map/while/body/eval_jaxpr/rgw,wd->rgd/dot_general | solution.py:72
  175.8 0.2 and_and_fusion.2
  176.1 2.1 fusion.43
  178.1 1.0 fusion.44
  179.1 2.6 %fusion.45 = bf16[8,128,8,128]{3,1,2,0:T(8,128)(2,1)} fusion(bf16[8,128,8,128]{3,1,2,0:T(8,128)(2,1)} %get-tuple-element.200, s32[]{:T(128)S(6)} %copy.43, f32[128,8,1152]{2,0,1:T(8,128)S(1)} %get-tuple-element.186, f32[128,8]{0,1:T(8,128)S(1)} %get-tuple-element.187, bf16[8,1152,128]{1,2,0:T(8,128)(2,1)} %get-tuple-element.214, ...), kind=kOutput, calls=%fused_computation.11.clone.1 | convolution fusion | flops 304611328 | bytes 5284864 | tf_op jit(solution)/shard_map/while/body/eval_jaxpr/rgw,wd->rgd/dot_general | solution.py:72
  181.7 0.2 and_and_fusion.2
  182.0 2.1 fusion.43
  184.0 1.0 fusion.44
  185.1 2.6 %fusion.45 = bf16[8,128,8,128]{3,1,2,0:T(8,128)(2,1)} fusion(bf16[8,128,8,128]{3,1,2,0:T(8,128)(2,1)} %get-tuple-element.200, s32[]{:T(128)S(6)} %copy.43, f32[128,8,1152]{2,0,1:T(8,128)S(1)} %get-tuple-element.186, f32[128,8]{0,1:T(8,128)S(1)} %get-tuple-element.187, bf16[8,1152,128]{1,2,0:T(8,128)(2,1)} %get-tuple-element.214, ...), kind=kOutput, calls=%fused_computation.11.clone.1 | convolution fusion | flops 304611328 | bytes 5284864 | tf_op jit(solution)/shard_map/while/body/eval_jaxpr/rgw,wd->rgd/dot_general | solution.py:72
  187.7 0.2 and_and_fusion.2
  187.9 2.1 fusion.43
  190.0 1.0 fusion.44
  191.0 2.6 %fusion.45 = bf16[8,128,8,128]{3,1,2,0:T(8,128)(2,1)} fusion(bf16[8,128,8,128]{3,1,2,0:T(8,128)(2,1)} %get-tuple-element.200, s32[]{:T(128)S(6)} %copy.43, f32[128,8,1152]{2,0,1:T(8,128)S(1)} %get-tuple-element.186, f32[128,8]{0,1:T(8,128)S(1)} %get-tuple-element.187, bf16[8,1152,128]{1,2,0:T(8,128)(2,1)} %get-tuple-element.214, ...), kind=kOutput, calls=%fused_computation.11.clone.1 | convolution fusion | flops 304611328 | bytes 5284864 | tf_op jit(solution)/shard_map/while/body/eval_jaxpr/rgw,wd->rgd/dot_general | solution.py:72
  193.6 0.2 and_and_fusion.2
  193.8 2.1 fusion.43
  195.9 1.0 fusion.44
  196.9 2.6 %fusion.45 = bf16[8,128,8,128]{3,1,2,0:T(8,128)(2,1)} fusion(bf16[8,128,8,128]{3,1,2,0:T(8,128)(2,1)} %get-tuple-element.200, s32[]{:T(128)S(6)} %copy.43, f32[128,8,1152]{2,0,1:T(8,128)S(1)} %get-tuple-element.186, f32[128,8]{0,1:T(8,128)S(1)} %get-tuple-element.187, bf16[8,1152,128]{1,2,0:T(8,128)(2,1)} %get-tuple-element.214, ...), kind=kOutput, calls=%fused_computation.11.clone.1 | convolution fusion | flops 304611328 | bytes 5284864 | tf_op jit(solution)/shard_map/while/body/eval_jaxpr/rgw,wd->rgd/dot_general | solution.py:72
  199.5 0.2 and_and_fusion.2
  199.7 2.1 fusion.43
  201.8 1.0 fusion.44
  202.8 2.6 %fusion.45 = bf16[8,128,8,128]{3,1,2,0:T(8,128)(2,1)} fusion(bf16[8,128,8,128]{3,1,2,0:T(8,128)(2,1)} %get-tuple-element.200, s32[]{:T(128)S(6)} %copy.43, f32[128,8,1152]{2,0,1:T(8,128)S(1)} %get-tuple-element.186, f32[128,8]{0,1:T(8,128)S(1)} %get-tuple-element.187, bf16[8,1152,128]{1,2,0:T(8,128)(2,1)} %get-tuple-element.214, ...), kind=kOutput, calls=%fused_computation.11.clone.1 | convolution fusion | flops 304611328 | bytes 5284864 | tf_op jit(solution)/shard_map/while/body/eval_jaxpr/rgw,wd->rgd/dot_general | solution.py:72
  205.4 0.2 and_and_fusion.2
  205.6 2.1 fusion.43
  207.7 1.0 fusion.44
  208.7 2.6 %fusion.45 = bf16[8,128,8,128]{3,1,2,0:T(8,128)(2,1)} fusion(bf16[8,128,8,128]{3,1,2,0:T(8,128)(2,1)} %get-tuple-element.200, s32[]{:T(128)S(6)} %copy.43, f32[128,8,1152]{2,0,1:T(8,128)S(1)} %get-tuple-element.186, f32[128,8]{0,1:T(8,128)S(1)} %get-tuple-element.187, bf16[8,1152,128]{1,2,0:T(8,128)(2,1)} %get-tuple-element.214, ...), kind=kOutput, calls=%fused_computation.11.clone.1 | convolution fusion | flops 304611328 | bytes 5284864 | tf_op jit(solution)/shard_map/while/body/eval_jaxpr/rgw,wd->rgd/dot_general | solution.py:72
  211.3 0.2 and_and_fusion.2
  211.5 2.1 fusion.43
  213.6 1.0 fusion.44
  214.6 2.6 %fusion.45 = bf16[8,128,8,128]{3,1,2,0:T(8,128)(2,1)} fusion(bf16[8,128,8,128]{3,1,2,0:T(8,128)(2,1)} %get-tuple-element.200, s32[]{:T(128)S(6)} %copy.43, f32[128,8,1152]{2,0,1:T(8,128)S(1)} %get-tuple-element.186, f32[128,8]{0,1:T(8,128)S(1)} %get-tuple-element.187, bf16[8,1152,128]{1,2,0:T(8,128)(2,1)} %get-tuple-element.214, ...), kind=kOutput, calls=%fused_computation.11.clone.1 | convolution fusion | flops 304611328 | bytes 5284864 | tf_op jit(solution)/shard_map/while/body/eval_jaxpr/rgw,wd->rgd/dot_general | solution.py:72
  217.2 2.9 %copy.22 = bf16[128,8,8,128]{3,2,1,0:T(8,128)(2,1)S(1)} copy(bf16[128,8,8,128]{3,0,2,1:T(8,128)(2,1)} %bitcast.52) | data formatting | bytes 4194304 | tf_op jit(solution)/shard_map/transpose | solution.py:76
  220.1 2.3 %broadcast_in_dim_reshape.3 = bf16[1,128,8192]{2,1,0:T(8,128)(2,1)} reshape(bf16[128,8,8,128]{3,2,1,0:T(8,128)(2,1)S(1)} %copy.22) | data formatting | bytes 4194304 | tf_op jit(solution)/shard_map/broadcast_in_dim;reshape | solution.py:96
  (28 shorter events, 1.5 us)
Async XLA Ops:
  14.6 32.5 %collective-permute-start = (bf16[2,128,1024]{1,2,0:T(8,128)(2,1)S(1)}, bf16[2,128,1024]{1,2,0:T(8,128)(2,1)}, u32[]{:S(2)}, u32[]{:S(2)}) collective-permute-start(bf16[2,128,1024]{1,2,0:T(8,128)(2,1)S(1)} %all_gather.3), channel_id=1, source_target_pairs={{0,8},{1,9},{2,10},{3,11},{4,12},{5,13},{6,14},{7,15},{8,16},{9,17... | collective-permute-start | bytes 1572872 | tf_op jit(solution)/shard_map/ppermute | solution.py:17
  15.9 50.9 %collective-permute-start.1 = (bf16[2,128,1024]{1,2,0:T(8,128)(2,1)S(1)}, bf16[2,128,1024]{1,2,0:T(8,128)(2,1)S(1)}, u32[]{:S(2)}, u32[]{:S(2)}) collective-permute-start(bf16[2,128,1024]{1,2,0:T(8,128)(2,1)S(1)} %all_gather.3), channel_id=1, source_target_pairs={{0,7},{1,8},{2,9},{3,10},{4,11},{5,12},{6,13},{7,14},{8,15},{9,16}... | collective-permute-start | bytes 1572872 | tf_op jit(solution)/shard_map/ppermute | solution.py:17
  21.0 69.8 %collective-permute-start.2 = (bf16[2,128,1024]{1,2,0:T(8,128)(2,1)S(1)}, bf16[2,128,1024]{1,2,0:T(8,128)(2,1)S(1)}, u32[]{:S(2)}, u32[]{:S(2)}) collective-permute-start(bf16[2,128,1024]{1,2,0:T(8,128)(2,1)S(1)} %all_gather.3), channel_id=1, source_target_pairs={{0,6},{1,7},{2,8},{3,9},{4,10},{5,11},{6,12},{7,13},{8,14},{9,15},... | collective-permute-start | bytes 1572872 | tf_op jit(solution)/shard_map/ppermute | solution.py:17
  22.9 90.0 %collective-permute-start.3 = (bf16[2,128,1024]{1,2,0:T(8,128)(2,1)S(1)}, bf16[2,128,1024]{1,2,0:T(8,128)(2,1)S(1)}, u32[]{:S(2)}, u32[]{:S(2)}) collective-permute-start(bf16[2,128,1024]{1,2,0:T(8,128)(2,1)S(1)} %all_gather.3), channel_id=1, source_target_pairs={{0,5},{1,6},{2,7},{3,8},{4,9},{5,10},{6,11},{7,12},{8,13},{9,14},{... | collective-permute-start | bytes 1572872 | tf_op jit(solution)/shard_map/ppermute | solution.py:17
  24.9 88.2 %collective-permute-start.4 = (bf16[2,128,1024]{1,2,0:T(8,128)(2,1)S(1)}, bf16[2,128,1024]{1,2,0:T(8,128)(2,1)S(1)}, u32[]{:S(2)}, u32[]{:S(2)}) collective-permute-start(bf16[2,128,1024]{1,2,0:T(8,128)(2,1)S(1)} %all_gather.3), channel_id=1, source_target_pairs={{0,4},{1,5},{2,6},{3,7},{4,8},{5,9},{6,10},{7,11},{8,12},{9,13},{1... | collective-permute-start | bytes 1572872 | tf_op jit(solution)/shard_map/ppermute | solution.py:17
  29.5 4.6 %copy-start.1 = (f32[1,64]{1,0:T(1,128)S(1)}, f32[1,64]{1,0:T(1,128)}, u32[]{:S(2)}) copy-start(f32[1,64]{1,0:T(1,128)} %param.8) | copy-start | bytes 772
  29.6 4.6 %copy-start = (s32[16]{0:T(128)S(1)}, s32[16]{0:T(128)}, u32[]{:S(2)}) copy-start(s32[16]{0:T(128)} %param.9) | copy-start | bytes 196
  47.1 72.9 %collective-permute-start.5 = (bf16[2,128,1024]{1,2,0:T(8,128)(2,1)S(1)}, bf16[2,128,1024]{1,2,0:T(8,128)(2,1)S(1)}, u32[]{:S(2)}, u32[]{:S(2)}) collective-permute-start(bf16[2,128,1024]{1,2,0:T(8,128)(2,1)S(1)} %all_gather.3), channel_id=1, source_target_pairs={{0,3},{1,4},{2,5},{3,6},{4,7},{5,8},{6,9},{7,10},{8,11},{9,12},{10... | collective-permute-start | bytes 1572872 | tf_op jit(solution)/shard_map/ppermute | solution.py:17
  66.7 68.0 %collective-permute-start.6 = (bf16[2,128,1024]{1,2,0:T(8,128)(2,1)S(1)}, bf16[2,128,1024]{1,2,0:T(8,128)(2,1)S(1)}, u32[]{:S(2)}, u32[]{:S(2)}) collective-permute-start(bf16[2,128,1024]{1,2,0:T(8,128)(2,1)S(1)} %all_gather.3), channel_id=1, source_target_pairs={{0,2},{1,3},{2,4},{3,5},{4,6},{5,7},{6,8},{7,9},{8,10},{9,11},{10,... | collective-permute-start | bytes 1572872 | tf_op jit(solution)/shard_map/ppermute | solution.py:17
  90.8 75.9 %collective-permute-start.7 = (bf16[2,128,1024]{1,2,0:T(8,128)(2,1)S(1)}, bf16[2,128,1024]{1,2,0:T(8,128)(2,1)S(1)}, u32[]{:S(2)}, u32[]{:S(2)}) collective-permute-start(bf16[2,128,1024]{1,2,0:T(8,128)(2,1)S(1)} %all_gather.3), channel_id=1, source_target_pairs={{0,1},{1,2},{2,3},{3,4},{4,5},{5,6},{6,7},{7,8},{8,9},{9,10},{10,1... | collective-permute-start | bytes 1572872 | tf_op jit(solution)/shard_map/ppermute | solution.py:17
where the time goes:
time: 223 us; the launch traced here: 222 us
  waiting for transfers between devices  112 us (50%)
  matrix products  37.5 us (17%)
  other arithmetic  25.7 us (12%)
  starting transfers between devices  18.1 us (8%)
  local copies, waits for them, and re-layouts  15.5 us (7%)
  blocking collectives  13.6 us (6%)
    ppermute x8, waiting for transfers between devices, passed_along(): lax.ppermute(value, axis, [(source, source + steps) for source in range(f...  112 us
    dot_general x8, matrix products, per_group(): jnp.einsum('rgw,wd->rgd', weights, v_part, preferred_element_type=jnp.flo...  20.8 us
    ppermute x8, starting transfers between devices, passed_along(): lax.ppermute(value, axis, [(source, source + steps) for source in range(f...  18.1 us
    dot_general x8, matrix products, per_group(): jnp.einsum('rgd,wd->rgw', q_part, k_part, preferred_element_type=jnp.floa...  16.7 us
    all_gather x1, blocking collectives, on_device(): whole = lax.all_gather(keys_values, 'cand', axis=2, tiled=True)  13.6 us
    another operation x4, other arithmetic  9.14 us
    reduce_sum x8, other arithmetic, per_group(): total = jnp.sum(expw, axis=-1, keepdims=True)  8.08 us
    slice x1, local copies, waits for them, and re-layouts, rotate(): first_half = shaped[..., :half_dim]  4.58 us
  transfers between devices with their start and end apart: 8, of which 6 were waited for; matrix products, arithmetic and copies ran while one was open for 10% of the time, Pallas kernels for 0%

commit v1 on v0

--- a/solution.py
+++ b/solution.py
@@ -81,7 +81,9 @@
     device = lax.axis_index("doc")
     query_index = device * row_count + jnp.arange(row_count, dtype=jnp.int32)
     key_index = (device - SPAN) * row_count + jnp.arange((SPAN + 1) * row_count, dtype=jnp.int32)
-    whole = lax.all_gather(keys_values, "cand", axis=2, tiled=True)
+    whole = jnp.concatenate(
+        lax.all_to_all(jnp.stack([keys_values] * lax.axis_size("cand")), "cand", 0, 0), axis=2
+    )
     pieces = []
     for distance in range(SPAN, 0, -1):
         pieces.append(passed_along(whole, "doc", distance))

time: 223 us -> 234 us (1.049)
  blocking collectives: 13.6 us -> 0 us
  waiting for transfers between devices: 112 us -> 120 us
  starting transfers between devices: 18.1 us -> 25.4 us
  local copies, waits for them, and re-layouts: 15.5 us -> 20.7 us
  other arithmetic: 25.7 us -> 28.5 us
    all_gather x1 -> x0, blocking collectives: 13.6 us -> none  [on_device(): whole = lax.all_gather(keys_values, 'cand', axis=2, tiled=True)]
    ppermute x8, waiting for transfers between devices: 112 us -> 120 us  [passed_along(): lax.ppermute(value, axis, [(source, source + steps) for source in range(f...]
    all_to_all x0 -> x1, starting transfers between devices: none -> 4.47 us  [on_device(): lax.all_to_all(jnp.stack([keys_values] * lax.axis_size('cand')), 'cand',...]
    unnamed x14, local copies, waits for them, and re-layouts: 3.71 us -> 7.87 us
    ppermute x8, starting transfers between devices: 18.1 us -> 20.9 us  [passed_along(): lax.ppermute(value, axis, [(source, source + steps) for source in range(f...]
  transfers between devices with their start and end apart: 8 -> 9, of which waited for: 6 -> 7; matrix products, arithmetic and copies ran while one was open for 10% -> 13% of each run, Pallas kernels for 0% -> 0%
where the time goes in v1:
time: 234 us; the launch traced here: 233 us
  waiting for transfers between devices  120 us (51%)
  matrix products  37.5 us (16%)
  other arithmetic  28.5 us (12%)
  starting transfers between devices  25.4 us (11%)
  local copies, waits for them, and re-layouts  20.7 us (9%)
    ppermute x8, waiting for transfers between devices, passed_along(): lax.ppermute(value, axis, [(source, source + steps) for source in range(f...  120 us
    ppermute x8, starting transfers between devices, passed_along(): lax.ppermute(value, axis, [(source, source + steps) for source in range(f...  20.9 us
    dot_general x8, matrix products, per_group(): jnp.einsum('rgw,wd->rgd', weights, v_part, preferred_element_type=jnp.flo...  20.8 us
    dot_general x8, matrix products, per_group(): jnp.einsum('rgd,wd->rgw', q_part, k_part, preferred_element_type=jnp.floa...  16.7 us
    another operation x4, other arithmetic  10.5 us
    reduce_sum x8, other arithmetic, per_group(): total = jnp.sum(expw, axis=-1, keepdims=True)  8.08 us
    unnamed x14, local copies, waits for them, and re-layouts  7.87 us
  transfers between devices with their start and end apart: 9, of which 7 were waited for; matrix products, arithmetic and copies ran while one was open for 13% of the time, Pallas kernels for 0%

profile of v1, /device:TPU:448, one launch (start us, length us, event | category | flops | bytes accessed | tf_op | source)
XLA Modules:
  0.0 232.8 jit_solution(14266993190634364751)
XLA Ops:
  0.0 0.9 copy.27
  1.0 1.0 stack.2
  1.9 4.5 %all-to-all-start = ((bf16[8,2,128,128]{2,3,1,0:T(8,128)(2,1)}), bf16[8,2,128,128]{2,3,1,0:T(8,128)(2,1)S(1)}, u32[]{:S(2)}, u32[]{:S(2)}) async-start(bf16[8,2,128,128]{2,3,1,0:T(8,128)(2,1)} %stack.2), calls=%async_computation | async-start | bytes 1048576 | tf_op jit(solution)/shard_map/all_to_all | solution.py:85
  6.4 2.0 convert_bitcast_fusion
  8.4 0.7 copy.36
  9.2 4.6 %fusion.35 = (f32[128,64,64]{2,1,0:T(8,128)}, f32[128,64,64]{2,1,0:T(8,128)}) fusion(f32[128,64,128]{2,1,0:T(8,128)S(1)} %bitcast.51), kind=kLoop, calls=%fused_computation.60 | loop fusion | bytes 8388608 | tf_op jit(solution)/shard_map/slice | solution.py:39
  14.4 0.3 multiply_cosine_fusion.1
  14.7 9.7 %subtract_convert_fusion = (bf16[128,64,64]{2,0,1:T(8,128)(2,1)S(1)}, bf16[128,64,64]{2,0,1:T(8,128)(2,1)}) fusion(f32[128,64,64]{2,1,0:T(8,128)} %get-tuple-element.126, f32[128,64,64]{2,1,0:T(8,128)} %get-tuple-element.125, f32[128,64]{1,0:T(8,128)S(1)} %get-tuple-element.130, f32[128,64]{1,0:T(8,128)S(1)} %get-tuple-element.129), kind=kLoop, calls=%fused_computation.23 | loop fusion | flops 4194304 | bytes 6356992 | tf_op jit(solution)/shard_map/convert.4
  24.4 1.3 collective-permute-start
  25.7 5.1 %collective-permute-start.1 = (bf16[2,128,1024]{1,2,0:T(8,128)(2,1)S(1)}, bf16[2,128,1024]{1,2,0:T(8,128)(2,1)}, u32[]{:S(2)}, u32[]{:S(2)}) collective-permute-start(bf16[2,128,1024]{1,2,0:T(8,128)(2,1)S(1)} %bitcast.57), channel_id=1, source_target_pairs={{0,7},{1,8},{2,9},{3,10},{4,11},{5,12},{6,13},{7,14},{8,15},{9,16}... | collective-permute-start | bytes 1572872 | tf_op jit(solution)/shard_map/ppermute | solution.py:17
  30.9 1.1 multiply_cosine_fusion
  32.0 1.9 collective-permute-start.2
  33.9 1.9 collective-permute-start.3
  35.8 1.9 collective-permute-start.4
  37.8 4.1 %pad_maximum_fusion = bf16[128,64,128]{2,0,1:T(8,128)(2,1)} fusion(bf16[128,64,64]{2,0,1:T(8,128)(2,1)} %get-tuple-element.120, bf16[128,64,64]{2,0,1:T(8,128)(2,1)S(1)} %get-tuple-element.119), kind=kLoop, calls=%fused_computation.27 | loop fusion | flops 4194304 | bytes 4194304 | tf_op jit(solution)/shard_map/concatenate | solution.py:41
  41.8 1.9 collective-permute-done
  43.7 4.7 %collective-permute-start.5 = (bf16[2,128,1024]{1,2,0:T(8,128)(2,1)S(1)}, bf16[2,128,1024]{1,2,0:T(8,128)(2,1)S(1)}, u32[]{:S(2)}, u32[]{:S(2)}) collective-permute-start(bf16[2,128,1024]{1,2,0:T(8,128)(2,1)S(1)} %bitcast.61), channel_id=1, source_target_pairs={{0,3},{1,4},{2,5},{3,6},{4,7},{5,8},{6,9},{7,10},{8,11},{9,12},{10... | collective-permute-start | bytes 1572872 | tf_op jit(solution)/shard_map/ppermute | solution.py:17
  48.4 1.1 constant_dynamic-update-slice_fusion.8
  49.6 27.1 %collective-permute-done.1 = bf16[2,128,1024]{1,2,0:T(8,128)(2,1)} collective-permute-done((bf16[2,128,1024]{1,2,0:T(8,128)(2,1)S(1)}, bf16[2,128,1024]{1,2,0:T(8,128)(2,1)}, u32[]{:S(2)}, u32[]{:S(2)}) %collective-permute-start.1) | collective-permute-done | bytes 524320 | tf_op jit(solution)/shard_map/ppermute | solution.py:17
  76.7 1.9 collective-permute-start.6
  78.6 1.2 constant_dynamic-update-slice_fusion.7
  79.8 20.9 %collective-permute-done.2 = bf16[2,128,1024]{1,2,0:T(8,128)(2,1)} collective-permute-done((bf16[2,128,1024]{1,2,0:T(8,128)(2,1)S(1)}, bf16[2,128,1024]{1,2,0:T(8,128)(2,1)}, u32[]{:S(2)}, u32[]{:S(2)}) %collective-permute-start.2) | collective-permute-done | bytes 524320 | tf_op jit(solution)/shard_map/ppermute | solution.py:17
  100.7 2.1 collective-permute-start.7
  102.8 1.2 constant_dynamic-update-slice_fusion.6
  104.0 18.9 %collective-permute-done.3 = bf16[2,128,1024]{1,2,0:T(8,128)(2,1)} collective-permute-done((bf16[2,128,1024]{1,2,0:T(8,128)(2,1)S(1)}, bf16[2,128,1024]{1,2,0:T(8,128)(2,1)}, u32[]{:S(2)}, u32[]{:S(2)}) %collective-permute-start.3) | collective-permute-done | bytes 524320 | tf_op jit(solution)/shard_map/ppermute | solution.py:17
  122.9 1.2 constant_dynamic-update-slice_fusion.5
  124.1 1.2 constant_dynamic-update-slice_fusion.4
  125.3 5.0 %collective-permute-done.5 = bf16[2,128,1024]{1,2,0:T(8,128)(2,1)S(1)} collective-permute-done((bf16[2,128,1024]{1,2,0:T(8,128)(2,1)S(1)}, bf16[2,128,1024]{1,2,0:T(8,128)(2,1)S(1)}, u32[]{:S(2)}, u32[]{:S(2)}) %collective-permute-start.5) | collective-permute-done | bytes 524320 | tf_op jit(solution)/shard_map/ppermute | solution.py:17
  130.4 14.4 %collective-permute-done.6 = bf16[2,128,1024]{1,2,0:T(8,128)(2,1)S(1)} collective-permute-done((bf16[2,128,1024]{1,2,0:T(8,128)(2,1)S(1)}, bf16[2,128,1024]{1,2,0:T(8,128)(2,1)S(1)}, u32[]{:S(2)}, u32[]{:S(2)}) %collective-permute-start.6) | collective-permute-done | bytes 524320 | tf_op jit(solution)/shard_map/ppermute | solution.py:17
  144.9 32.1 %collective-permute-done.7 = bf16[2,128,1024]{1,2,0:T(8,128)(2,1)S(1)} collective-permute-done((bf16[2,128,1024]{1,2,0:T(8,128)(2,1)S(1)}, bf16[2,128,1024]{1,2,0:T(8,128)(2,1)S(1)}, u32[]{:S(2)}, u32[]{:S(2)}) %collective-permute-start.7) | collective-permute-done | bytes 524320 | tf_op jit(solution)/shard_map/ppermute | solution.py:17
  177.3 1.8 fusion.34
  179.1 0.3 convert.18
  179.4 0.6 subtract_convert_fusion.1
  180.0 0.2 maximum_bitcast_fusion
  180.2 47.3 %while.11 = (s32[]{:T(128)}, bf16[8,128,8,128]{3,1,2,0:T(8,128)(2,1)}, bf16[8,128,8,128]{3,1,2,0:T(8,128)(2,1)}, bf16[8,1152,128]{1,2,0:T(8,128)(2,1)S(1)}, bf16...) while((s32[]{:T(128)}, ...), condition=%wide.region_8.9_spmd.clone, body=%wide.region_5.8_spmd.clone.sunk | while | flops 613087232 | bytes 15598837 | solution.py:75
  180.3 0.2 and_and_fusion.2
  180.5 2.1 fusion.43
  182.6 1.0 fusion.44
  183.6 2.6 %fusion.45 = bf16[8,128,8,128]{3,1,2,0:T(8,128)(2,1)} fusion(bf16[8,128,8,128]{3,1,2,0:T(8,128)(2,1)} %get-tuple-element.210, s32[]{:T(128)S(6)} %copy.52, f32[128,8,1152]{2,0,1:T(8,128)S(1)} %get-tuple-element.196, f32[128,8]{0,1:T(8,128)S(1)} %get-tuple-element.197, bf16[8,1152,128]{1,2,0:T(8,128)(2,1)} %get-tuple-element.224, ...), kind=kOutput, calls=%fused_computation.11.clone.1 | convolution fusion | flops 304611328 | bytes 5284864 | tf_op jit(solution)/shard_map/while/body/eval_jaxpr/rgw,wd->rgd/dot_general | solution.py:72
  186.2 0.2 and_and_fusion.2
  186.4 2.1 fusion.43
  188.5 1.0 fusion.44
  189.5 2.6 %fusion.45 = bf16[8,128,8,128]{3,1,2,0:T(8,128)(2,1)} fusion(bf16[8,128,8,128]{3,1,2,0:T(8,128)(2,1)} %get-tuple-element.210, s32[]{:T(128)S(6)} %copy.52, f32[128,8,1152]{2,0,1:T(8,128)S(1)} %get-tuple-element.196, f32[128,8]{0,1:T(8,128)S(1)} %get-tuple-element.197, bf16[8,1152,128]{1,2,0:T(8,128)(2,1)} %get-tuple-element.224, ...), kind=kOutput, calls=%fused_computation.11.clone.1 | convolution fusion | flops 304611328 | bytes 5284864 | tf_op jit(solution)/shard_map/while/body/eval_jaxpr/rgw,wd->rgd/dot_general | solution.py:72
  192.1 0.2 and_and_fusion.2
  192.3 2.1 fusion.43
  194.4 1.0 fusion.44
  195.4 2.6 %fusion.45 = bf16[8,128,8,128]{3,1,2,0:T(8,128)(2,1)} fusion(bf16[8,128,8,128]{3,1,2,0:T(8,128)(2,1)} %get-tuple-element.210, s32[]{:T(128)S(6)} %copy.52, f32[128,8,1152]{2,0,1:T(8,128)S(1)} %get-tuple-element.196, f32[128,8]{0,1:T(8,128)S(1)} %get-tuple-element.197, bf16[8,1152,128]{1,2,0:T(8,128)(2,1)} %get-tuple-element.224, ...), kind=kOutput, calls=%fused_computation.11.clone.1 | convolution fusion | flops 304611328 | bytes 5284864 | tf_op jit(solution)/shard_map/while/body/eval_jaxpr/rgw,wd->rgd/dot_general | solution.py:72
  198.2 2.1 fusion.43
  200.3 1.0 fusion.44
  201.3 2.6 %fusion.45 = bf16[8,128,8,128]{3,1,2,0:T(8,128)(2,1)} fusion(bf16[8,128,8,128]{3,1,2,0:T(8,128)(2,1)} %get-tuple-element.210, s32[]{:T(128)S(6)} %copy.52, f32[128,8,1152]{2,0,1:T(8,128)S(1)} %get-tuple-element.196, f32[128,8]{0,1:T(8,128)S(1)} %get-tuple-element.197, bf16[8,1152,128]{1,2,0:T(8,128)(2,1)} %get-tuple-element.224, ...), kind=kOutput, calls=%fused_computation.11.clone.1 | convolution fusion | flops 304611328 | bytes 5284864 | tf_op jit(solution)/shard_map/while/body/eval_jaxpr/rgw,wd->rgd/dot_general | solution.py:72
  204.1 2.1 fusion.43
  206.2 1.0 fusion.44
  207.2 2.6 %fusion.45 = bf16[8,128,8,128]{3,1,2,0:T(8,128)(2,1)} fusion(bf16[8,128,8,128]{3,1,2,0:T(8,128)(2,1)} %get-tuple-element.210, s32[]{:T(128)S(6)} %copy.52, f32[128,8,1152]{2,0,1:T(8,128)S(1)} %get-tuple-element.196, f32[128,8]{0,1:T(8,128)S(1)} %get-tuple-element.197, bf16[8,1152,128]{1,2,0:T(8,128)(2,1)} %get-tuple-element.224, ...), kind=kOutput, calls=%fused_computation.11.clone.1 | convolution fusion | flops 304611328 | bytes 5284864 | tf_op jit(solution)/shard_map/while/body/eval_jaxpr/rgw,wd->rgd/dot_general | solution.py:72
  210.0 2.1 fusion.43
  212.1 1.0 fusion.44
  213.1 2.6 %fusion.45 = bf16[8,128,8,128]{3,1,2,0:T(8,128)(2,1)} fusion(bf16[8,128,8,128]{3,1,2,0:T(8,128)(2,1)} %get-tuple-element.210, s32[]{:T(128)S(6)} %copy.52, f32[128,8,1152]{2,0,1:T(8,128)S(1)} %get-tuple-element.196, f32[128,8]{0,1:T(8,128)S(1)} %get-tuple-element.197, bf16[8,1152,128]{1,2,0:T(8,128)(2,1)} %get-tuple-element.224, ...), kind=kOutput, calls=%fused_computation.11.clone.1 | convolution fusion | flops 304611328 | bytes 5284864 | tf_op jit(solution)/shard_map/while/body/eval_jaxpr/rgw,wd->rgd/dot_general | solution.py:72
  215.9 2.1 fusion.43
  218.0 1.0 fusion.44
  219.0 2.6 %fusion.45 = bf16[8,128,8,128]{3,1,2,0:T(8,128)(2,1)} fusion(bf16[8,128,8,128]{3,1,2,0:T(8,128)(2,1)} %get-tuple-element.210, s32[]{:T(128)S(6)} %copy.52, f32[128,8,1152]{2,0,1:T(8,128)S(1)} %get-tuple-element.196, f32[128,8]{0,1:T(8,128)S(1)} %get-tuple-element.197, bf16[8,1152,128]{1,2,0:T(8,128)(2,1)} %get-tuple-element.224, ...), kind=kOutput, calls=%fused_computation.11.clone.1 | convolution fusion | flops 304611328 | bytes 5284864 | tf_op jit(solution)/shard_map/while/body/eval_jaxpr/rgw,wd->rgd/dot_general | solution.py:72
  221.8 2.1 fusion.43
  223.9 1.0 fusion.44
  224.9 2.6 %fusion.45 = bf16[8,128,8,128]{3,1,2,0:T(8,128)(2,1)} fusion(bf16[8,128,8,128]{3,1,2,0:T(8,128)(2,1)} %get-tuple-element.210, s32[]{:T(128)S(6)} %copy.52, f32[128,8,1152]{2,0,1:T(8,128)S(1)} %get-tuple-element.196, f32[128,8]{0,1:T(8,128)S(1)} %get-tuple-element.197, bf16[8,1152,128]{1,2,0:T(8,128)(2,1)} %get-tuple-element.224, ...), kind=kOutput, calls=%fused_computation.11.clone.1 | convolution fusion | flops 304611328 | bytes 5284864 | tf_op jit(solution)/shard_map/while/body/eval_jaxpr/rgw,wd->rgd/dot_general | solution.py:72
  227.5 2.9 %copy.31 = bf16[128,8,8,128]{3,2,1,0:T(8,128)(2,1)S(1)} copy(bf16[128,8,8,128]{3,0,2,1:T(8,128)(2,1)} %bitcast.55) | data formatting | bytes 4194304 | tf_op jit(solution)/shard_map/transpose | solution.py:76
  230.5 2.3 broadcast_in_dim_reshape.3
  (31 shorter events, 2.2 us)
Async XLA Ops:
  1.9 22.5 %all-to-all-start = ((bf16[8,2,128,128]{2,3,1,0:T(8,128)(2,1)}), bf16[8,2,128,128]{2,3,1,0:T(8,128)(2,1)S(1)}, u32[]{:S(2)}, u32[]{:S(2)}) async-start(bf16[8,2,128,128]{2,3,1,0:T(8,128)(2,1)} %stack.2), calls=%async_computation | async-start | bytes 1048576 | tf_op jit(solution)/shard_map/all_to_all | solution.py:85
  9.1 4.6 %copy-start.1 = (f32[1,64]{1,0:T(1,128)S(1)}, f32[1,64]{1,0:T(1,128)}, u32[]{:S(2)}) copy-start(f32[1,64]{1,0:T(1,128)} %param.8) | copy-start | bytes 772
  9.1 4.6 %copy-start = (s32[16]{0:T(128)S(1)}, s32[16]{0:T(128)}, u32[]{:S(2)}) copy-start(s32[16]{0:T(128)} %param.9) | copy-start | bytes 196
  24.4 19.3 %collective-permute-start = (bf16[2,128,1024]{1,2,0:T(8,128)(2,1)S(1)}, bf16[2,128,1024]{1,2,0:T(8,128)(2,1)}, u32[]{:S(2)}, u32[]{:S(2)}) collective-permute-start(bf16[2,128,1024]{1,2,0:T(8,128)(2,1)S(1)} %bitcast.56), channel_id=1, source_target_pairs={{0,8},{1,9},{2,10},{3,11},{4,12},{5,13},{6,14},{7,15},{8,16},{9,17... | collective-permute-start | bytes 1572872 | tf_op jit(solution)/shard_map/ppermute | solution.py:17
  25.7 51.0 %collective-permute-start.1 = (bf16[2,128,1024]{1,2,0:T(8,128)(2,1)S(1)}, bf16[2,128,1024]{1,2,0:T(8,128)(2,1)}, u32[]{:S(2)}, u32[]{:S(2)}) collective-permute-start(bf16[2,128,1024]{1,2,0:T(8,128)(2,1)S(1)} %bitcast.57), channel_id=1, source_target_pairs={{0,7},{1,8},{2,9},{3,10},{4,11},{5,12},{6,13},{7,14},{8,15},{9,16}... | collective-permute-start | bytes 1572872 | tf_op jit(solution)/shard_map/ppermute | solution.py:17
  32.0 68.8 %collective-permute-start.2 = (bf16[2,128,1024]{1,2,0:T(8,128)(2,1)S(1)}, bf16[2,128,1024]{1,2,0:T(8,128)(2,1)}, u32[]{:S(2)}, u32[]{:S(2)}) collective-permute-start(bf16[2,128,1024]{1,2,0:T(8,128)(2,1)S(1)} %bitcast.58), channel_id=1, source_target_pairs={{0,6},{1,7},{2,8},{3,9},{4,10},{5,11},{6,12},{7,13},{8,14},{9,15},... | collective-permute-start | bytes 1572872 | tf_op jit(solution)/shard_map/ppermute | solution.py:17
  33.9 89.0 %collective-permute-start.3 = (bf16[2,128,1024]{1,2,0:T(8,128)(2,1)S(1)}, bf16[2,128,1024]{1,2,0:T(8,128)(2,1)}, u32[]{:S(2)}, u32[]{:S(2)}) collective-permute-start(bf16[2,128,1024]{1,2,0:T(8,128)(2,1)S(1)} %bitcast.59), channel_id=1, source_target_pairs={{0,5},{1,6},{2,7},{3,8},{4,9},{5,10},{6,11},{7,12},{8,13},{9,14},{... | collective-permute-start | bytes 1572872 | tf_op jit(solution)/shard_map/ppermute | solution.py:17
  35.8 88.3 %collective-permute-start.4 = (bf16[2,128,1024]{1,2,0:T(8,128)(2,1)S(1)}, bf16[2,128,1024]{1,2,0:T(8,128)(2,1)}, u32[]{:S(2)}, u32[]{:S(2)}) collective-permute-start(bf16[2,128,1024]{1,2,0:T(8,128)(2,1)S(1)} %bitcast.60), channel_id=1, source_target_pairs={{0,4},{1,5},{2,6},{3,7},{4,8},{5,9},{6,10},{7,11},{8,12},{9,13},{1... | collective-permute-start | bytes 1572872 | tf_op jit(solution)/shard_map/ppermute | solution.py:17
  43.7 86.5 %collective-permute-start.5 = (bf16[2,128,1024]{1,2,0:T(8,128)(2,1)S(1)}, bf16[2,128,1024]{1,2,0:T(8,128)(2,1)S(1)}, u32[]{:S(2)}, u32[]{:S(2)}) collective-permute-start(bf16[2,128,1024]{1,2,0:T(8,128)(2,1)S(1)} %bitcast.61), channel_id=1, source_target_pairs={{0,3},{1,4},{2,5},{3,6},{4,7},{5,8},{6,9},{7,10},{8,11},{9,12},{10... | collective-permute-start | bytes 1572872 | tf_op jit(solution)/shard_map/ppermute | solution.py:17
  76.7 68.1 %collective-permute-start.6 = (bf16[2,128,1024]{1,2,0:T(8,128)(2,1)S(1)}, bf16[2,128,1024]{1,2,0:T(8,128)(2,1)S(1)}, u32[]{:S(2)}, u32[]{:S(2)}) collective-permute-start(bf16[2,128,1024]{1,2,0:T(8,128)(2,1)S(1)} %bitcast.62), channel_id=1, source_target_pairs={{0,2},{1,3},{2,4},{3,5},{4,6},{5,7},{6,8},{7,9},{8,10},{9,11},{10,... | collective-permute-start | bytes 1572872 | tf_op jit(solution)/shard_map/ppermute | solution.py:17
  100.7 76.3 %collective-permute-start.7 = (bf16[2,128,1024]{1,2,0:T(8,128)(2,1)S(1)}, bf16[2,128,1024]{1,2,0:T(8,128)(2,1)S(1)}, u32[]{:S(2)}, u32[]{:S(2)}) collective-permute-start(bf16[2,128,1024]{1,2,0:T(8,128)(2,1)S(1)} %bitcast.63), channel_id=1, source_target_pairs={{0,1},{1,2},{2,3},{3,4},{4,5},{5,6},{6,7},{7,8},{8,9},{9,10},{10,1... | collective-permute-start | bytes 1572872 | tf_op jit(solution)/shard_map/ppermute | solution.py:17
